TPU v7x, 512 devices: a whole 4x4x16 slice. The times are simulated.
512 devices in a mesh: fsdp: 32 (over x_lo, z), tp: 16 (over x_hi, y, core).
Axes of the slice: x: 4 (x_hi: 2, x_lo: 2; x = x_hi * 2 + x_lo), y: 4, z: 16, core: 2. Of those that a mesh axis runs over, the one named last changes fastest.
Arguments:
- activations: bfloat16 [16384, 4096], P(('fsdp', 'tp')), may hold values from -6 to 6
- norm_gain: float32 [4096], replicated, may hold values from 0.5 to 1.5
- proj_weight: bfloat16 [3, 4096, 4096], P(None, 'fsdp', 'tp'), may hold values from -0.09375 to 0.09375
- short_filter: float32 [256, 7], P('tp'), may hold values from -3 to 3
- segment_ids: int32 [32, 512], P('fsdp'), may hold values from 0 to 7, never falling along the last dimension, each value on 1 to 256 neighbouring positions
- needle_pos: int32 [32, 16], P('fsdp'), may hold values from 0 to 511
- readout: float32 [4096], replicated, may hold values from -6 to 6
Outputs:
- mixer_out: bfloat16 [16384, 4096], P(('fsdp', 'tp'))
- needle_score: float32 [32, 16], P('fsdp')
Inputs may be any that keep to these rules, and one draw needn't show every extreme that they name: segment_ids never fall along a slab; each document covers 1 to 256 positions.
All inputs are finite; a program needn't handle non-finite values.
Results may differ from a plain program's by a relative error of at most 0.0068.
Values may be sent and summed in bfloat16 or wider, within the bound.
No kernel may reach another device: no remote copies, remote signals or barrier semaphores. Data moves between devices by JAX's collectives and lax.ppermute only.
A program may use at most 64 MiB of HBM per device.

v0:
```python
import math
import jax
import jax.numpy as jnp
from jax import lax
from jax.sharding import PartitionSpec as P

EPSILON = 1e-06


def short_conv(gated_prod, tap_table, segments):
    length = gated_prod.shape[0]
    filtered = jnp.zeros(gated_prod.shape, jnp.float32)
    for offset in range(tap_table.shape[1]):
        shifted = jnp.pad(gated_prod, ((offset, 0), (0, 0)))[:length]
        earlier = jnp.pad(segments, (offset, 0), constant_values=-1)[:length]
        same_doc = (earlier == segments).astype(jnp.float32)
        filtered = filtered + shifted * same_doc[:, None] * tap_table[:, offset][None, :]
    return filtered


def local(activations, norm_gain, proj_weight, short_filter, segment_ids, needle_pos, readout):
    model_width = activations.shape[1]
    local_rows = activations.shape[0]
    values = activations.astype(jnp.float32)
    scaled = lax.rsqrt(jnp.mean(values * values, axis=1, keepdims=True) + EPSILON)
    normed = (values * scaled * norm_gain[None, :]).astype(jnp.bfloat16)
    slab_rows = lax.all_gather(normed, "tp", axis=0, tiled=True)
    channels = proj_weight.shape[2]
    projected = jnp.einsum(
        "sk,ikc->isc",
        slab_rows,
        lax.all_gather(proj_weight, "fsdp", axis=1, tiled=True),
        preferred_element_type=jnp.float32,
    )
    gated_prod = projected[1] * projected[2]
    tap_table = jnp.repeat(short_filter, channels // short_filter.shape[0], axis=0)
    filtered = short_conv(gated_prod, tap_table, segment_ids[0])
    mixed_local = (projected[0] * filtered).astype(jnp.bfloat16)
    device_rank = lax.axis_index("tp")
    full_rows = lax.all_gather(mixed_local, "tp", axis=1, tiled=True)
    own_rows = lax.dynamic_slice_in_dim(full_rows, device_rank * local_rows, local_rows, 0)
    positions = needle_pos[0]
    local_pos = positions - device_rank * local_rows
    picker = (local_pos[:, None] == jnp.arange(local_rows, dtype=jnp.int32)[None, :]).astype(
        jnp.bfloat16
    )
    picked = jnp.dot(picker, own_rows, preferred_element_type=jnp.float32)
    partial_sum = jnp.sum(picked * readout[None, :], axis=1)
    summed_score = lax.psum(partial_sum, "tp")
    needle_score = (summed_score / math.sqrt(model_width))[None, :]
    return (own_rows, needle_score)


def solution(mesh):
    in_specs = (
        P(("fsdp", "tp"), None),
        P(),
        P(None, "fsdp", "tp"),
        P("tp", None),
        P("fsdp", None),
        P("fsdp", None),
        P(),
    )
    out_specs = (P(("fsdp", "tp"), None), P("fsdp", None))
    return jax.shard_map(local, mesh=mesh, in_specs=in_specs, out_specs=out_specs, check_vma=False)
```

profile of v0, /device:TPU:1, one launch (start us, length us, event | category | flops | bytes accessed | tf_op | source)
XLA Modules:
  0.0 348.2 jit_solution(14428492473865925798)
XLA Ops:
  7.2 0.0 all-gather.4.cloned.1.call-start
  7.2 1.1 fusion.26
  8.3 1.8 fusion.28
  10.1 0.0 all-gather.4.cloned.1.call-update
  10.1 0.0 all-gather.6.cloned.1.call-start
  10.2 0.7 all-gather.6.cloned.1.call-update
  10.9 0.0 all-gather.8.cloned.1.call-start
  10.9 0.8 broadcast_in_dim.4
  11.7 0.1 reshape.38
  11.8 1.0 fusion.42
  12.8 0.0 copy-start.2
  12.8 0.0 copy-start.1
  12.9 75.4 %all-gather.4.cloned.1.call-done = bf16[512,4096]{1,0:T(8,128)(2,1)} async-done(((bf16[32,4096]{1,0:T(8,128)(2,1)}), bf16[512,4096]{1,0:T(8,128)(2,1)}) %all-gather.4.cloned.1.call-update) | async-done | bytes 4194320 | tf_op jit(solution)/shard_map/all_gather | solution.py:27
  88.3 123.8 %all-gather.6.cloned.1.call-done = bf16[3,4096,256]{2,1,0:T(8,128)(2,1)} async-done(((bf16[3,128,256]{2,1,0:T(8,128)(2,1)}), bf16[3,4096,256]{2,1,0:T(8,128)(2,1)}) %all-gather.6.cloned.1.call-update) | async-done | bytes 6291472 | tf_op jit(solution)/shard_map/all_gather | solution.py:32
  212.0 7.0 %fusion.2 = f32[3,512,256]{2,1,0:T(8,128)S(1)} fusion(bf16[3,4096,256]{2,1,0:T(8,128)(2,1)} %all-gather.6.cloned.1.call-done, bf16[512,4096]{1,0:T(8,128)(2,1)} %all-gather.4.cloned.1.call-done), kind=kOutput, calls=%fused_computation.3 | convolution fusion | flops 3221225472 | bytes 12058624 | tf_op jit(solution)/shard_map/sk,ikc->isc/dot_general | solution.py:29
  219.1 0.1 fusion.29
  219.1 1.5 fusion.15
  220.6 0.0 all-gather.8.cloned.1.call-update
  220.6 0.0 copy-done.2
  220.7 86.4 %all-gather.8.cloned.1.call-done = bf16[512,4096]{1,0:T(8,128)(2,1)} async-done(((bf16[512,256]{1,0:T(8,128)(2,1)}), bf16[512,4096]{1,0:T(8,128)(2,1)}) %all-gather.8.cloned.1.call-update) | async-done | bytes 4194320 | tf_op jit(solution)/shard_map/all_gather | solution.py:40
  307.1 1.0 constant_dynamic-slice_fusion
  308.0 0.0 copy-done.1
  308.0 0.0 copy-start
  308.0 0.3 fusion.5
  308.4 32.8 %psum.7 = f32[16]{0:T(128)S(1)} all-reduce(f32[16]{0:T(128)S(1)} %fusion.5), channel_id=1, replica_groups=mesh['fsdp'=32,'tp'=16] {'tp'}, use_global_device_ids=true, to_apply=%region_2.3 | all-reduce | flops 16 | bytes 128 | tf_op jit(solution)/shard_map/psum | solution.py:49
  341.1 0.5 multiply_bitcast_fusion
  341.7 0.0 copy-done
  (3 shorter events, 0.0 us)
Async XLA Ops:
  7.2 81.1 %all-gather.4.cloned.1.call-start = ((), (), s32[]{:S(2)}) async-start(), calls=%async_computation | async-start | bytes 4456448 | tf_op jit(solution)/shard_map/all_gather | solution.py:27
  10.1 201.9 %all-gather.6.cloned.1.call-start = ((), (), s32[]{:S(2)}) async-start(), calls=%async_computation.1 | async-start | bytes 6488064 | tf_op jit(solution)/shard_map/all_gather | solution.py:32
  10.9 296.2 %all-gather.8.cloned.1.call-start = ((), (), s32[]{:S(2)}) async-start(), calls=%async_computation.2 | async-start | bytes 4456448 | tf_op jit(solution)/shard_map/all_gather | solution.py:40
  12.8 207.8 %copy-start.2 = (s32[1,16]{1,0:T(1,128)S(1)}, s32[1,16]{1,0:T(1,128)}, u32[]{:S(2)}) copy-start(s32[1,16]{1,0:T(1,128)} %param.12) | copy-start | bytes 196
  12.8 295.2 %copy-start.1 = (f32[4096]{0:T(1024)S(1)}, f32[4096]{0:T(1024)}, u32[]{:S(2)}) copy-start(f32[4096]{0:T(1024)} %param.13) | copy-start | bytes 49156
  308.0 33.6 %copy-start = (bf16[32,4096]{1,0:T(8,128)(2,1)}, bf16[32,4096]{1,0:T(8,128)(2,1)S(1)}, u32[]{:S(2)}) copy-start(bf16[32,4096]{1,0:T(8,128)(2,1)S(1)} %constant_dynamic-slice_fusion) | copy-start | bytes 786436
Sparse Core Ops, SparseCore 0:
  11.9 76.3 all-gather.3
  90.4 121.6 all-gather.5
  220.8 86.2 all-gather.7
where the time goes:
time: 348 us
  waiting for transfers between devices  286 us (82%)
  blocking collectives  32.8 us (9%)
  between operations  13.8 us (4%)
  matrix products  7.37 us (2%)
  other arithmetic  5.98 us (2%)
    all_gather x1, waiting for transfers between devices, local(): lax.all_gather(proj_weight, 'fsdp', axis=1, tiled=True)  124 us
    all_gather x1, waiting for transfers between devices, local(): full_rows = lax.all_gather(mixed_local, 'tp', axis=1, tiled=True)  86.4 us
    all_gather x1, waiting for transfers between devices, local(): slab_rows = lax.all_gather(normed, 'tp', axis=0, tiled=True)  75.4 us
    psum x1, blocking collectives, local(): summed_score = lax.psum(partial_sum, 'tp')  32.8 us
    dot_general x1, matrix products, local(): jnp.einsum('sk,ikc->isc', slab_rows, lax.all_gather(proj_weight, 'fsdp',...  7.03 us
  transfers between devices with their start and end apart: 3, of which 3 were waited for; matrix products, arithmetic and copies ran while one was open for 1% of the time, Pallas kernels for 0%

commit v1 on v0

--- a/solution.py
+++ b/solution.py
@@ -29,7 +29,9 @@
     projected = jnp.einsum(
         "sk,ikc->isc",
         slab_rows,
-        lax.all_gather(proj_weight, "fsdp", axis=1, tiled=True),
+        jnp.concatenate(
+            lax.all_to_all(jnp.stack([proj_weight] * lax.axis_size("fsdp")), "fsdp", 0, 0), axis=1
+        ),
         preferred_element_type=jnp.float32,
     )
     gated_prod = projected[1] * projected[2]

time: 348 us -> 431 us (1.24)
  waiting for transfers between devices: 286 us -> 345 us
  starting transfers between devices: 0.12 us -> 17.3 us
  local copies, waits for them, and re-layouts: 1.84 us -> 11.7 us
    all_to_all x0 -> x1, waiting for transfers between devices: none -> 272 us  [local(): lax.all_to_all(jnp.stack([proj_weight] * lax.axis_size('fsdp')), 'fsdp',...]
    all_gather x1 -> x0, waiting for transfers between devices: 124 us -> none  [local(): lax.all_gather(proj_weight, 'fsdp', axis=1, tiled=True)]
    all_gather x1, waiting for transfers between devices: 75.4 us -> 0.01 us  [local(): slab_rows = lax.all_gather(normed, 'tp', axis=0, tiled=True)]
    all_to_all x0 -> x1, starting transfers between devices: none -> 17.2 us  [local(): lax.all_to_all(jnp.stack([proj_weight] * lax.axis_size('fsdp')), 'fsdp',...]
    all_gather x1, waiting for transfers between devices: 86.4 us -> 72.5 us  [local(): full_rows = lax.all_gather(mixed_local, 'tp', axis=1, tiled=True)]
    reshape x0 -> x1, local copies, waits for them, and re-layouts: none -> 6.21 us  [local(): jnp.concatenate(lax.all_to_all(jnp.stack([proj_weight] * lax.axis_size('f...]
    another operation x0 -> x1, local copies, waits for them, and re-layouts: none -> 4.33 us  [local(): jnp.stack([proj_weight] * lax.axis_size('fsdp'))]
  transfers between devices with their start and end apart: 3 -> 3, of which waited for: 3 -> 2; matrix products, arithmetic and copies ran while one was open for 1% -> 2% of each run, Pallas kernels for 0% -> 0%
where the time goes in v1:
time: 431 us
  waiting for transfers between devices  345 us (80%)
  blocking collectives  32.8 us (8%)
  starting transfers between devices  17.3 us (4%)
  between operations  14.2 us (3%)
  local copies, waits for them, and re-layouts  11.7 us (3%)
  matrix products  7.39 us (2%)
    all_to_all x1, waiting for transfers between devices, local(): lax.all_to_all(jnp.stack([proj_weight] * lax.axis_size('fsdp')), 'fsdp',...  272 us
    all_gather x1, waiting for transfers between devices, local(): full_rows = lax.all_gather(mixed_local, 'tp', axis=1, tiled=True)  72.5 us
    psum x1, blocking collectives, local(): summed_score = lax.psum(partial_sum, 'tp')  32.8 us
    all_to_all x1, starting transfers between devices, local(): lax.all_to_all(jnp.stack([proj_weight] * lax.axis_size('fsdp')), 'fsdp',...  17.2 us
  transfers between devices with their start and end apart: 3, of which 2 were waited for; matrix products, arithmetic and copies ran while one was open for 2% of the time, Pallas kernels for 0%

profile of v1, /device:TPU:1, one launch (start us, length us, event | category | flops | bytes accessed | tf_op | source)
XLA Modules:
  0.0 431.2 jit_solution(14965672320211528066)
XLA Ops:
  7.2 4.3 %stack.2 = bf16[32,3,128,256]{3,2,1,0:T(8,128)(2,1)} broadcast(bf16[3,128,256]{2,1,0:T(8,128)(2,1)} %param.9), dimensions={1,2,3} | broadcast | bytes 6488064 | tf_op jit(solution)/shard_map/stack | solution.py:33
  11.5 0.0 copy-start
  11.5 0.0 copy-start.2
  11.5 0.0 copy-start.3
  11.5 0.0 copy-start.4
  11.5 17.2 %all-to-all-start = ((bf16[32,3,128,256]{3,2,1,0:T(8,128)(2,1)}), bf16[32,3,128,256]{3,2,1,0:T(8,128)(2,1)}, u32[]{:S(2)}, u32[]{:S(2)}) async-start(bf16[32,3,128,256]{3,2,1,0:T(8,128)(2,1)} %stack.2), calls=%async_computation | async-start | bytes 12582912 | tf_op jit(solution)/shard_map/all_to_all | solution.py:33
  28.7 0.0 all-gather.3.cloned.1.call-start
  28.8 0.0 copy-done
  28.8 0.2 fusion.26
  29.0 0.0 copy-done.2
  29.0 0.8 fusion.28
  29.8 0.0 all-gather.3.cloned.1.call-update
  29.8 0.0 all-gather.5.cloned.1.call-start
  29.9 0.0 copy-done.3
  29.9 0.1 broadcast_in_dim.4
  30.0 0.1 reshape.48
  30.1 0.0 copy-done.4
  30.1 0.1 fusion.42
  30.2 272.3 %all-to-all-done = bf16[32,3,128,256]{3,2,1,0:T(8,128)(2,1)} async-done(((bf16[32,3,128,256]{3,2,1,0:T(8,128)(2,1)}), bf16[32,3,128,256]{3,2,1,0:T(8,128)(2,1)}, u32[]{:S(2)}, u32[]{:S(2)}) %all-to-all-start) | async-done | bytes 6291488 | tf_op jit(solution)/shard_map/all_to_all | solution.py:33
  302.4 6.2 %copy.10 = bf16[3,32,128,256]{3,2,1,0:T(8,128)(2,1)} copy(bf16[3,32,128,256]{3,2,0,1:T(8,128)(2,1)} %bitcast.1) | data formatting | bytes 12582912 | tf_op jit(solution)/shard_map/reshape | solution.py:32
  308.6 0.0 all-gather.3.cloned.1.call-done
  308.6 0.0 copy-start.6
  308.6 0.0 copy-start.5
  308.6 7.1 %fusion.2 = f32[3,512,256]{2,1,0:T(8,128)S(1)} fusion(bf16[3,4096,256]{2,1,0:T(8,128)(2,1)} %bitcast.31, bf16[512,4096]{1,0:T(8,128)(2,1)} %all-gather.3.cloned.1.call-done), kind=kOutput, calls=%fused_computation.3 | convolution fusion | flops 3221225472 | bytes 12058624 | tf_op jit(solution)/shard_map/sk,ikc->isc/dot_general | solution.py:29
  315.7 0.1 fusion.29
  315.8 1.5 fusion.15
  317.2 0.0 all-gather.5.cloned.1.call-update
  317.3 0.0 copy-done.6
  317.3 72.5 %all-gather.5.cloned.1.call-done = bf16[512,4096]{1,0:T(8,128)(2,1)} async-done(((bf16[512,256]{1,0:T(8,128)(2,1)}), bf16[512,4096]{1,0:T(8,128)(2,1)}) %all-gather.5.cloned.1.call-update) | async-done | bytes 4194320 | tf_op jit(solution)/shard_map/all_gather | solution.py:42
  389.7 1.0 constant_dynamic-slice_fusion
  390.7 0.0 copy-done.5
  390.7 0.0 copy-start.1
  390.7 0.3 fusion.5
  391.1 32.8 %psum.7 = f32[16]{0:T(128)S(1)} all-reduce(f32[16]{0:T(128)S(1)} %fusion.5), channel_id=1, replica_groups=mesh['fsdp'=32,'tp'=16] {'tp'}, use_global_device_ids=true, to_apply=%region_2.3 | all-reduce | flops 16 | bytes 128 | tf_op jit(solution)/shard_map/psum | solution.py:51
  423.8 0.5 multiply_bitcast_fusion
  424.4 0.0 copy-done.1
  (3 shorter events, 0.0 us)
Async XLA Ops:
  11.5 17.3 %copy-start = (bf16[32,4096]{1,0:T(8,128)(2,1)S(1)}, bf16[32,4096]{1,0:T(8,128)(2,1)}, u32[]{:S(2)}) copy-start(bf16[32,4096]{1,0:T(8,128)(2,1)} %param.7) | copy-start | bytes 786436
  11.5 17.5 %copy-start.2 = (f32[4096]{0:T(1024)S(1)}, f32[4096]{0:T(1024)}, u32[]{:S(2)}) copy-start(f32[4096]{0:T(1024)} %param.8) | copy-start | bytes 49156
  11.5 18.4 %copy-start.3 = (f32[16,7]{0,1:T(8,128)S(1)}, f32[16,7]{0,1:T(8,128)}, u32[]{:S(2)}) copy-start(f32[16,7]{0,1:T(8,128)} %param.10) | copy-start | bytes 1348
  11.5 18.6 %copy-start.4 = (s32[1,512]{1,0:T(1,128)S(1)}, s32[1,512]{1,0:T(1,128)}, u32[]{:S(2)}) copy-start(s32[1,512]{1,0:T(1,128)} %param.11) | copy-start | bytes 6148
  11.5 290.9 %all-to-all-start = ((bf16[32,3,128,256]{3,2,1,0:T(8,128)(2,1)}), bf16[32,3,128,256]{3,2,1,0:T(8,128)(2,1)}, u32[]{:S(2)}, u32[]{:S(2)}) async-start(bf16[32,3,128,256]{3,2,1,0:T(8,128)(2,1)} %stack.2), calls=%async_computation | async-start | bytes 12582912 | tf_op jit(solution)/shard_map/all_to_all | solution.py:33
  28.7 279.9 %all-gather.3.cloned.1.call-start = ((), (), s32[]{:S(2)}) async-start(), calls=%async_computation.1 | async-start | bytes 4456448 | tf_op jit(solution)/shard_map/all_gather | solution.py:27
  29.8 359.9 %all-gather.5.cloned.1.call-start = ((), (), s32[]{:S(2)}) async-start(), calls=%async_computation.2 | async-start | bytes 4456448 | tf_op jit(solution)/shard_map/all_gather | solution.py:42
  308.6 8.6 %copy-start.6 = (s32[1,16]{1,0:T(1,128)S(1)}, s32[1,16]{1,0:T(1,128)}, u32[]{:S(2)}) copy-start(s32[1,16]{1,0:T(1,128)} %param.12) | copy-start | bytes 196
  308.6 82.1 %copy-start.5 = (f32[4096]{0:T(1024)S(1)}, f32[4096]{0:T(1024)}, u32[]{:S(2)}) copy-start(f32[4096]{0:T(1024)} %param.13) | copy-start | bytes 49156
  390.7 33.6 %copy-start.1 = (bf16[32,4096]{1,0:T(8,128)(2,1)}, bf16[32,4096]{1,0:T(8,128)(2,1)S(1)}, u32[]{:S(2)}) copy-start(bf16[32,4096]{1,0:T(8,128)(2,1)S(1)} %constant_dynamic-slice_fusion) | copy-start | bytes 786436
Sparse Core Ops, SparseCore 0:
  33.5 76.8 all-gather.2
  317.4 72.3 all-gather.4
